TPU v7x, 128 devices: a whole 4x4x4 slice. The times are simulated.
128 devices in a mesh: blk: 16 (over y_hi, x, core), reg: 8 (over z, y_lo).
Axes of the slice: x: 4, y: 4 (y_hi: 2, y_lo: 2; y = y_hi * 2 + y_lo), z: 4, core: 2. Of those that a mesh axis runs over, the one named last changes fastest.
Arguments:
- inv_factor: bfloat16 [256, 1024, 1024], P(('blk', 'reg')), may hold values from -0.1875 to 0.1875
- border_global: bfloat16 [256, 1024, 512], P(('blk', 'reg')), may hold values from -6 to 6
- border_local: bfloat16 [256, 1024, 1536], P(('blk', 'reg')), may hold values from -6 to 6
- local_count: int32 [256], P(('blk', 'reg')), may hold values from 512 to 1536, as said below
Outputs:
- schur_global: float32 [512, 512], P('blk')
- schur_local: float32 [8, 1536, 1536], P('reg', 'blk')
- schur_cross: float32 [8, 512, 1536], P('reg', 'blk')
Inputs may be any that keep to these rules, and one draw needn't show every extreme that they name: Each block touches the first local_count of its region's local linking columns; some block touches exactly 1536 and some exactly 512.
All inputs are finite; a program needn't handle non-finite values.
Results may differ from a plain program's by a relative error of at most 0.0039.
Values may be sent and summed in bfloat16 or wider, within the bound.
No kernel may reach another device: no remote copies, remote signals or barrier semaphores. Data moves between devices by JAX's collectives and lax.ppermute only.
A program may use at most 128 MiB of HBM per device.

v0:
```python
import math
import jax
import jax.numpy as jnp
import numpy as np
from jax import lax
from jax.sharding import Mesh
from jax.sharding import PartitionSpec as P

BLK_AXES = ("yh", "x", "core")
REG_AXES = ("z", "yl")
CHIP_AXES = ("yh", "x")


def left_products(factor, border):
    return lax.dot_general(
        factor, border, (((1,), (1,)), ((0,), (0,))), preferred_element_type=jnp.float32
    ).astype(jnp.bfloat16)


def gram(first, second):
    return lax.dot_general(
        first, second, (((0,), (0,)), ((), ())), preferred_element_type=jnp.float32
    )


def owner_major(left, n_chip, n_core):
    rows, cols = left.shape
    per = cols // (n_chip * n_core)
    return left.reshape(rows, n_chip, n_core, per).transpose(0, 2, 1, 3).reshape(rows, cols)


def shards(inv_factor, border_global, border_local, local_count):
    blk_dev, order, _ = inv_factor.shape
    global_cols = border_global.shape[2]
    local_cols = border_local.shape[2]
    n_core = lax.axis_size("core")
    n_chip = lax.axis_size("yh") * lax.axis_size("x")
    n_blk = n_core * n_chip
    n_reg = lax.axis_size("z") * lax.axis_size("yl")
    columns = jnp.arange(local_cols, dtype=jnp.int32)
    masked = jnp.where(
        columns[None, None, :] < local_count[:, None, None],
        border_local,
        jnp.zeros((), border_local.dtype),
    )
    left_g = left_products(inv_factor, border_global).reshape(blk_dev * order, global_cols)
    left_l = left_products(inv_factor, masked).reshape(blk_dev * order, local_cols)
    part_top = gram(owner_major(left_g, n_chip, n_core), jnp.concatenate([left_g, left_l], axis=1))
    part_ll = gram(owner_major(left_l, n_chip, n_core), left_l)
    rows_g = global_cols // n_blk
    rows_l = local_cols // n_blk
    top = part_top.reshape(n_core, n_chip * rows_g, global_cols + local_cols)
    low = part_ll.reshape(n_core, n_chip * rows_l, local_cols)
    top = lax.psum_scatter(top, "core", scatter_dimension=0, tiled=True)
    low = lax.psum_scatter(low, "core", scatter_dimension=0, tiled=True)
    top = top.reshape(n_chip, rows_g * (global_cols + local_cols))
    low = low.reshape(n_chip, rows_l * local_cols)
    send = jnp.concatenate([top, low], axis=1).astype(jnp.bfloat16)
    got = lax.all_to_all(send, CHIP_AXES, 0, 0, tiled=True)
    summed = jnp.sum(got.astype(jnp.float32), axis=0)
    split = rows_g * (global_cols + local_cols)
    top = summed[:split].reshape(rows_g, global_cols + local_cols)
    low = summed[split:].reshape(rows_l, local_cols)
    all_blocks = blk_dev * n_blk * n_reg
    global_scale = 1.0 / math.sqrt(order * all_blocks)
    region_scale = 1.0 / math.sqrt(order * blk_dev * n_blk)
    global_part = lax.psum(top[:, :global_cols], REG_AXES)
    return (
        global_part * global_scale,
        (low * region_scale)[None],
        (top[:, global_cols:] * region_scale)[None],
    )


def solution(mesh):
    n_blk, n_reg = mesh.devices.shape
    devices = np.asarray(mesh.devices).reshape(2, n_blk // 4, 2, n_reg // 2, 2)
    fine = Mesh(devices, BLK_AXES + REG_AXES)
    every = BLK_AXES + REG_AXES
    placed = (P(every, None, None), P(every, None, None), P(every, None, None), P(every))
    return jax.shard_map(
        shards,
        mesh=fine,
        in_specs=placed,
        out_specs=(P(BLK_AXES, None), P(REG_AXES, BLK_AXES, None), P(REG_AXES, BLK_AXES, None)),
        check_vma=False,
    )
```

profile of v0, /device:TPU:0, one launch (start us, length us, event | category | flops | bytes accessed | tf_op | source)
XLA Modules:
  0.0 317.8 jit_solution(14593690149484430413)
XLA Ops:
  7.2 0.0 copy-start
  7.2 0.0 reduce-scatter.3.cloned.1.call-start
  7.2 0.9 iota_compare_fusion
  8.1 0.7 copy-done
  8.8 5.9 %convolution_convert_fusion = bf16[2,1024,512]{2,1,0:T(8,128)(2,1)} fusion(bf16[2,1024,1024]{2,1,0:T(8,128)(2,1)} %param.4, bf16[2,1024,512]{2,1,0:T(8,128)(2,1)S(1)} %copy-done), kind=kOutput, calls=%fused_computation.11 | convolution fusion | flops 2148532224 | bytes 8388608 | tf_op jit(solution)/shard_map/dot_general | solution.py:15
  14.7 6.3 %copy.16 = bf16[2,1024,512]{1,0,2:T(2,128)(2,1)} copy(bf16[2,1024,512]{2,1,0:T(8,128)(2,1)} %convolution_convert_fusion) | data formatting | bytes 4194304 | tf_op jit(solution)/shard_map/convert_element_type | solution.py:17
  21.0 3.3 %reshape_reshape.6 = bf16[2048,8,2,32]{0,3,2,1:T(8,128)(2,1)S(1)} reshape(bf16[2,1024,512]{1,0,2:T(2,128)(2,1)} %copy.16) | data formatting | bytes 4194304 | tf_op jit(solution)/shard_map/reshape;reshape | solution.py:29
  24.3 0.1 copy.17
  24.4 0.0 copy-start.3
  24.4 10.5 %fusion.6 = bf16[2,1536,1024]{1,2,0:T(8,128)(2,1)S(1)} fusion(bf16[2,1024,1024]{2,1,0:T(8,128)(2,1)} %param.4, bf16[2,1024,1536]{2,1,0:T(8,128)(2,1)} %param.6, pred[2,1536]{1,0:T(4,128)(4,1)S(1)} %iota_compare_fusion), kind=kOutput, calls=%fused_computation.9 | convolution fusion | flops 6448742400 | bytes 16780288 | tf_op jit(solution)/shard_map/dot_general | solution.py:15
  34.9 0.0 copy-start.2
  34.9 2.7 copy-done.2
  37.6 0.0 copy-done.3
  37.6 6.2 %fusion = f32[2,256,2048]{2,1,0:T(8,128)} fusion(bf16[2,256,2048]{2,1,0:T(8,128)(2,1)S(1)} %bitcast.40, bf16[2048,1536]{1,0:T(8,128)(2,1)S(1)} %bitcast.35, bf16[2048,512]{1,0:T(8,128)(2,1)S(1)} %bitcast.39), kind=kOutput, calls=%fused_computation.1 | convolution fusion | flops 4311744512 | bytes 14680064 | tf_op jit(solution)/shard_map/dot_general | solution.py:21
  43.8 0.0 reduce-scatter.3.cloned.1.call-update
  43.8 0.2 reduce-scatter.5.cloned.1.call-start
  44.1 16.7 %copy.19 = bf16[2,1024,1536]{1,0,2:T(2,128)(2,1)} copy(bf16[2,1024,1536]{2,1,0:T(8,128)(2,1)} %bitcast.36) | data formatting | bytes 12582912 | tf_op jit(solution)/shard_map/convert_element_type | solution.py:17
  60.8 11.1 %reshape_reshape.7 = bf16[2048,8,2,96]{0,3,2,1:T(8,128)(2,1)} reshape(bf16[2,1024,1536]{1,0,2:T(2,128)(2,1)} %copy.19) | data formatting | bytes 12582912 | tf_op jit(solution)/shard_map/reshape;reshape | solution.py:29
  71.9 3.4 %copy.20 = bf16[2048,2,8,96]{0,3,2,1:T(8,128)(2,1)S(1)} copy(bf16[2048,2,8,96]{0,3,1,2:T(8,128)(2,1)} %bitcast.33) | data formatting | bytes 12582912 | tf_op jit(solution)/shard_map/transpose | solution.py:29
  75.2 13.8 %fusion.13 = f32[2,768,1536]{2,1,0:T(8,128)} fusion(bf16[2,768,2048]{2,1,0:T(8,128)(2,1)S(1)} %bitcast.38, bf16[2048,1536,1]{1,0,2:T(8,128)(2,1)} %bitcast.37), kind=kOutput, calls=%fused_computation.19 | convolution fusion | flops 9663676416 | bytes 22020096 | tf_op jit(solution)/shard_map/dot_general | solution.py:21
  89.1 0.0 reduce-scatter.5.cloned.1.call-update
  89.1 0.0 all-reduce.2.cloned.1.call-start
  89.1 0.0 reduce-scatter.3.cloned.1.call-done
  89.2 1.7 convert.8
  90.9 1.7 concatenate.22
  92.6 19.1 %reduce-scatter.5.cloned.1.call-done = f32[1,768,1536]{2,1,0:T(8,128)} async-done(((f32[2,768,1536]{2,1,0:T(8,128)}), f32[1,768,1536]{2,1,0:T(8,128)}) %reduce-scatter.5.cloned.1.call-update) | async-done | bytes 4718608 | tf_op jit(solution)/shard_map/reduce_scatter | solution.py:55
  111.8 4.1 %convert.9 = bf16[1,768,1536]{2,1,0:T(8,128)(2,1)} convert(f32[1,768,1536]{2,1,0:T(8,128)} %reduce-scatter.5.cloned.1.call-done) | non-fusion elementwise | flops 1179648 | bytes 7077888 | tf_op jit(solution)/shard_map/convert.2
  115.9 6.6 %concatenate.23 = bf16[8,1,147456]{2,1,0:T(2,128)(2,1)} reshape(bf16[1,768,1536]{2,1,0:T(8,128)(2,1)} %convert.9) | data formatting | bytes 4718592 | tf_op jit(solution)/shard_map/concatenate | solution.py:58
  122.5 16.3 %pad_maximum_fusion = bf16[8,1,212992]{2,1,0:T(2,128)(2,1)} fusion(bf16[8,1,147456]{2,1,0:T(2,128)(2,1)} %concatenate.23, bf16[8,1,65536]{2,1,0:T(2,128)(2,1)S(1)} %concatenate.22), kind=kLoop, calls=%fused_computation.4 | loop fusion | flops 6815744 | bytes 6815744 | tf_op jit(solution)/shard_map/concatenate | solution.py:58
  138.8 0.5 broadcast.22
  139.3 23.5 %reduce.1 = bf16[8,212992]{1,0:T(8,128)(2,1)} reduce(bf16[8,1,212992]{2,1,0:T(2,128)(2,1)} %pad_maximum_fusion, bf16[]{:T(256)} %broadcast.22), dimensions={1}, to_apply=%pad_maximum_fusion.reduce_sub_computation | reduce | bytes 6815746 | tf_op jit(solution)/shard_map/concatenate | solution.py:58
  162.8 6.8 %reshape.109 = bf16[8,2,106496]{2,1,0:T(2,128)(2,1)} reshape(bf16[8,212992]{1,0:T(8,128)(2,1)} %reduce.1) | data formatting | bytes 6815744
  169.6 49.7 %all_to_all.6 = bf16[8,2,106496]{2,1,0:T(2,128)(2,1)} all-to-all(bf16[8,2,106496]{2,1,0:T(2,128)(2,1)} %reshape.109), channel_id=1, replica_groups=mesh['yh'=2,'x'=4,'core'=2,'z'=4,'yl'=2] {'yh','x'}, dimensions={0} | all-to-all | bytes 6815744 | tf_op jit(solution)/shard_map/all_to_all | solution.py:59
  219.3 0.0 copy-start.1
  219.3 8.2 %reshape.110 = bf16[8,1,212992]{2,1,0:T(2,128)(2,1)} reshape(bf16[8,2,106496]{2,1,0:T(2,128)(2,1)} %all_to_all.6) | data formatting | bytes 6815744
  227.6 10.0 %convert_reduce_fusion = f32[212992]{0:T(1024)S(1)} fusion(bf16[8,1,212992]{2,1,0:T(2,128)(2,1)} %reshape.110), kind=kLoop, calls=%fused_computation.5 | loop fusion | flops 3194880 | bytes 4259840 | tf_op jit(solution)/shard_map/reduce_sum | solution.py:60
  237.6 0.1 slice_multiply_fusion
  237.7 0.6 slice.28
  238.4 0.0 all-reduce.2.cloned.1.call-update
  238.4 0.7 fusion.10
  239.1 0.9 mul.32
  240.0 69.8 %all-reduce.2.cloned.1.call-done = f32[32,512]{1,0:T(8,128)} async-done(((f32[32,512]{1,0:T(8,128)}), f32[32,512]{1,0:T(8,128)}) %all-reduce.2.cloned.1.call-update) | async-done | bytes 65552 | tf_op jit(solution)/shard_map/psum | solution.py:67
  309.8 1.5 broadcast_multiply_fusion
  311.2 0.0 copy-done.1
  (2 shorter events, 0.1 us)
Async XLA Ops:
  7.2 1.6 copy-start
  7.2 82.0 %reduce-scatter.3.cloned.1.call-start = ((), (), s32[]{:S(2)}) async-start(), calls=%async_computation.3 | async-start | bytes 6291456 | tf_op jit(solution)/shard_map/reduce_scatter | solution.py:54
  24.4 13.2 %copy-start.3 = (bf16[2,1024,512]{2,1,0:T(8,128)(2,1)S(1)}, bf16[2,1024,512]{2,1,0:T(8,128)(2,1)}, u32[]{:S(2)}) copy-start(bf16[2,1024,512]{2,1,0:T(8,128)(2,1)} %convolution_convert_fusion) | copy-start | bytes 6291460
  34.9 2.7 copy-start.2
  43.8 67.9 %reduce-scatter.5.cloned.1.call-start = ((), (), s32[]{:S(2)}) async-start(), calls=%async_computation.4 | async-start | bytes 14155776 | tf_op jit(solution)/shard_map/reduce_scatter | solution.py:55
  89.1 220.7 %all-reduce.2.cloned.1.call-start = ((), (), s32[]{:S(2)}) async-start(), calls=%async_computation.5 | async-start | bytes 131072 | tf_op jit(solution)/shard_map/psum | solution.py:67
  219.3 91.9 %copy-start.1 = (bf16[2,1024,512]{2,1,0:T(8,128)(2,1)S(1)}, bf16[2,1024,512]{2,1,0:T(8,128)(2,1)}, u32[]{:S(2)}) copy-start(bf16[2,1024,512]{2,1,0:T(8,128)(2,1)} %param.5) | copy-start | bytes 6291460
Sparse Core Ops, SparseCore 0:
  44.0 17.2 reduce-scatter.2
  89.2 22.5 reduce-scatter.4
  238.5 71.2 all-reduce.1
where the time goes:
time: 319 us; the launch traced here: 318 us
  waiting for transfers between devices  89 us (28%)
  local copies, waits for them, and re-layouts  69.7 us (22%)
  other arithmetic  58.8 us (18%)
  blocking collectives  49.7 us (16%)
  matrix products  36.5 us (11%)
  between operations  13.9 us (4%)
    psum x1, waiting for transfers between devices, shards(): global_part = lax.psum(top[:, :global_cols], REG_AXES)  69.8 us
    all_to_all x1, blocking collectives, shards(): got = lax.all_to_all(send, CHIP_AXES, 0, 0, tiled=True)  49.7 us
    concatenate x2, other arithmetic, shards(): send = jnp.concatenate([top, low], axis=1).astype(jnp.bfloat16)  39.8 us
    convert_element_type x2, local copies, waits for them, and re-layouts, left_products(): return lax.dot_general(factor, border, (((1,), (1,)), ((0,), (0,))), pref...  23 us
    dot_general x2, matrix products, gram(): lax.dot_general(first, second, (((0,), (0,)), ((), ())), preferred_elemen...  20.1 us
    reduce_scatter x1, waiting for transfers between devices, shards(): low = lax.psum_scatter(low, 'core', scatter_dimension=0, tiled=True)  19.1 us
    unnamed x10, local copies, waits for them, and re-layouts  18.4 us
    dot_general x2, matrix products, left_products(): lax.dot_general(factor, border, (((1,), (1,)), ((0,), (0,))), preferred_e...  16.4 us
  transfers between devices with their start and end apart: 3, of which 2 were waited for; matrix products, arithmetic and copies ran while one was open for 16% of the time, Pallas kernels for 0%

commit v1 on v0

--- a/solution.py
+++ b/solution.py
@@ -64,7 +64,7 @@
     all_blocks = blk_dev * n_blk * n_reg
     global_scale = 1.0 / math.sqrt(order * all_blocks)
     region_scale = 1.0 / math.sqrt(order * blk_dev * n_blk)
-    global_part = lax.psum(top[:, :global_cols], REG_AXES)
+    global_part = jnp.sum(lax.all_gather(top[:, :global_cols], REG_AXES), axis=0)
     return (
         global_part * global_scale,
         (low * region_scale)[None],

time: 319 us -> 279 us (0.87)
  waiting for transfers between devices: 89 us -> 19.2 us
  blocking collectives: 49.7 us -> 80.1 us
    psum x1 -> x0, waiting for transfers between devices: 69.8 us -> none  [shards(): global_part = lax.psum(top[:, :global_cols], REG_AXES)]
    all_gather x0 -> x1, blocking collectives: none -> 30.4 us  [shards(): lax.all_gather(top[:, :global_cols], REG_AXES)]
  transfers between devices with their start and end apart: 3 -> 2, of which waited for: 2 -> 1; matrix products, arithmetic and copies ran while one was open for 16% -> 17% of each run, Pallas kernels for 0% -> 0%
where the time goes in v1:
time: 279 us; the launch traced here: 277 us
  blocking collectives  80.1 us (29%)
  local copies, waits for them, and re-layouts  69 us (25%)
  other arithmetic  58 us (21%)
  matrix products  36.5 us (13%)
  waiting for transfers between devices  19.2 us (7%)
  between operations  14.2 us (5%)
    all_to_all x1, blocking collectives, shards(): got = lax.all_to_all(send, CHIP_AXES, 0, 0, tiled=True)  49.7 us
    concatenate x2, other arithmetic, shards(): send = jnp.concatenate([top, low], axis=1).astype(jnp.bfloat16)  39.8 us
    all_gather x1, blocking collectives, shards(): lax.all_gather(top[:, :global_cols], REG_AXES)  30.4 us
    convert_element_type x2, local copies, waits for them, and re-layouts, left_products(): return lax.dot_general(factor, border, (((1,), (1,)), ((0,), (0,))), pref...  23 us
    dot_general x2, matrix products, gram(): lax.dot_general(first, second, (((0,), (0,)), ((), ())), preferred_elemen...  20.1 us
    reduce_scatter x1, waiting for transfers between devices, shards(): low = lax.psum_scatter(low, 'core', scatter_dimension=0, tiled=True)  19.2 us
    unnamed x10, local copies, waits for them, and re-layouts  18.4 us
    dot_general x2, matrix products, left_products(): lax.dot_general(factor, border, (((1,), (1,)), ((0,), (0,))), preferred_e...  16.4 us
  transfers between devices with their start and end apart: 2, of which 1 were waited for; matrix products, arithmetic and copies ran while one was open for 17% of the time, Pallas kernels for 0%

profile of v1, /device:TPU:0, one launch (start us, length us, event | category | flops | bytes accessed | tf_op | source)
XLA Modules:
  0.0 277.3 jit_solution(18078613678904243139)
XLA Ops:
  7.2 0.0 copy-start
  7.2 0.0 reduce-scatter.3.cloned.1.call-start
  7.2 0.9 iota_compare_fusion
  8.1 0.7 copy-done
  8.8 5.9 %convolution_convert_fusion = bf16[2,1024,512]{2,1,0:T(8,128)(2,1)} fusion(bf16[2,1024,1024]{2,1,0:T(8,128)(2,1)} %param.4, bf16[2,1024,512]{2,1,0:T(8,128)(2,1)S(1)} %copy-done), kind=kOutput, calls=%fused_computation.11 | convolution fusion | flops 2148532224 | bytes 8388608 | tf_op jit(solution)/shard_map/dot_general | solution.py:15
  14.7 6.3 %copy.16 = bf16[2,1024,512]{1,0,2:T(2,128)(2,1)} copy(bf16[2,1024,512]{2,1,0:T(8,128)(2,1)} %convolution_convert_fusion) | data formatting | bytes 4194304 | tf_op jit(solution)/shard_map/convert_element_type | solution.py:17
  21.0 3.3 %reshape_reshape.6 = bf16[2048,8,2,32]{0,3,2,1:T(8,128)(2,1)S(1)} reshape(bf16[2,1024,512]{1,0,2:T(2,128)(2,1)} %copy.16) | data formatting | bytes 4194304 | tf_op jit(solution)/shard_map/reshape;reshape | solution.py:29
  24.3 0.1 copy.17
  24.4 0.0 copy-start.3
  24.4 10.5 %fusion.6 = bf16[2,1536,1024]{1,2,0:T(8,128)(2,1)S(1)} fusion(bf16[2,1024,1024]{2,1,0:T(8,128)(2,1)} %param.4, bf16[2,1024,1536]{2,1,0:T(8,128)(2,1)} %param.6, pred[2,1536]{1,0:T(4,128)(4,1)S(1)} %iota_compare_fusion), kind=kOutput, calls=%fused_computation.9 | convolution fusion | flops 6448742400 | bytes 16780288 | tf_op jit(solution)/shard_map/dot_general | solution.py:15
  34.9 0.0 copy-start.2
  34.9 2.7 copy-done.2
  37.6 0.0 copy-done.3
  37.6 6.2 %fusion = f32[2,256,2048]{2,1,0:T(8,128)} fusion(bf16[2,256,2048]{2,1,0:T(8,128)(2,1)S(1)} %bitcast.41, bf16[2048,1536]{1,0:T(8,128)(2,1)S(1)} %bitcast.36, bf16[2048,512]{1,0:T(8,128)(2,1)S(1)} %bitcast.40), kind=kOutput, calls=%fused_computation.1 | convolution fusion | flops 4311744512 | bytes 14680064 | tf_op jit(solution)/shard_map/dot_general | solution.py:21
  43.8 0.0 reduce-scatter.3.cloned.1.call-update
  43.8 0.2 reduce-scatter.5.cloned.1.call-start
  44.1 16.7 %copy.19 = bf16[2,1024,1536]{1,0,2:T(2,128)(2,1)} copy(bf16[2,1024,1536]{2,1,0:T(8,128)(2,1)} %bitcast.37) | data formatting | bytes 12582912 | tf_op jit(solution)/shard_map/convert_element_type | solution.py:17
  60.8 11.1 %reshape_reshape.7 = bf16[2048,8,2,96]{0,3,2,1:T(8,128)(2,1)} reshape(bf16[2,1024,1536]{1,0,2:T(2,128)(2,1)} %copy.19) | data formatting | bytes 12582912 | tf_op jit(solution)/shard_map/reshape;reshape | solution.py:29
  71.9 3.4 %copy.20 = bf16[2048,2,8,96]{0,3,2,1:T(8,128)(2,1)S(1)} copy(bf16[2048,2,8,96]{0,3,1,2:T(8,128)(2,1)} %bitcast.34) | data formatting | bytes 12582912 | tf_op jit(solution)/shard_map/transpose | solution.py:29
  75.2 13.8 %fusion.13 = f32[2,768,1536]{2,1,0:T(8,128)} fusion(bf16[2,768,2048]{2,1,0:T(8,128)(2,1)S(1)} %bitcast.39, bf16[2048,1536,1]{1,0,2:T(8,128)(2,1)} %bitcast.38), kind=kOutput, calls=%fused_computation.19 | convolution fusion | flops 9663676416 | bytes 22020096 | tf_op jit(solution)/shard_map/dot_general | solution.py:21
  89.1 0.0 reduce-scatter.5.cloned.1.call-update
  89.1 0.0 reduce-scatter.3.cloned.1.call-done
  89.1 1.7 convert.8
  90.8 1.7 concatenate.22
  92.6 19.2 %reduce-scatter.5.cloned.1.call-done = f32[1,768,1536]{2,1,0:T(8,128)} async-done(((f32[2,768,1536]{2,1,0:T(8,128)}), f32[1,768,1536]{2,1,0:T(8,128)}) %reduce-scatter.5.cloned.1.call-update) | async-done | bytes 4718608 | tf_op jit(solution)/shard_map/reduce_scatter | solution.py:55
  111.8 4.1 %convert.9 = bf16[1,768,1536]{2,1,0:T(8,128)(2,1)} convert(f32[1,768,1536]{2,1,0:T(8,128)} %reduce-scatter.5.cloned.1.call-done) | non-fusion elementwise | flops 1179648 | bytes 7077888 | tf_op jit(solution)/shard_map/convert.2
  115.9 6.6 %concatenate.23 = bf16[8,1,147456]{2,1,0:T(2,128)(2,1)} reshape(bf16[1,768,1536]{2,1,0:T(8,128)(2,1)} %convert.9) | data formatting | bytes 4718592 | tf_op jit(solution)/shard_map/concatenate | solution.py:58
  122.5 16.3 %pad_maximum_fusion = bf16[8,1,212992]{2,1,0:T(2,128)(2,1)} fusion(bf16[8,1,147456]{2,1,0:T(2,128)(2,1)} %concatenate.23, bf16[8,1,65536]{2,1,0:T(2,128)(2,1)S(1)} %concatenate.22), kind=kLoop, calls=%fused_computation.4 | loop fusion | flops 6815744 | bytes 6815744 | tf_op jit(solution)/shard_map/concatenate | solution.py:58
  138.8 0.5 broadcast.22
  139.3 23.5 %reduce.1 = bf16[8,212992]{1,0:T(8,128)(2,1)} reduce(bf16[8,1,212992]{2,1,0:T(2,128)(2,1)} %pad_maximum_fusion, bf16[]{:T(256)} %broadcast.22), dimensions={1}, to_apply=%pad_maximum_fusion.reduce_sub_computation | reduce | bytes 6815746 | tf_op jit(solution)/shard_map/concatenate | solution.py:58
  162.8 6.8 %reshape.110 = bf16[8,2,106496]{2,1,0:T(2,128)(2,1)} reshape(bf16[8,212992]{1,0:T(8,128)(2,1)} %reduce.1) | data formatting | bytes 6815744
  169.6 49.7 %all_to_all.6 = bf16[8,2,106496]{2,1,0:T(2,128)(2,1)} all-to-all(bf16[8,2,106496]{2,1,0:T(2,128)(2,1)} %reshape.110), channel_id=1, replica_groups=mesh['yh'=2,'x'=4,'core'=2,'z'=4,'yl'=2] {'yh','x'}, dimensions={0} | all-to-all | bytes 6815744 | tf_op jit(solution)/shard_map/all_to_all | solution.py:59
  219.3 0.0 copy-start.1
  219.3 8.2 %reshape.111 = bf16[8,1,212992]{2,1,0:T(2,128)(2,1)} reshape(bf16[8,2,106496]{2,1,0:T(2,128)(2,1)} %all_to_all.6) | data formatting | bytes 6815744
  227.6 10.0 %convert_reduce_fusion = f32[212992]{0:T(1024)S(1)} fusion(bf16[8,1,212992]{2,1,0:T(2,128)(2,1)} %reshape.111), kind=kLoop, calls=%fused_computation.5 | loop fusion | flops 3194880 | bytes 4259840 | tf_op jit(solution)/shard_map/reduce_sum | solution.py:60
  237.7 0.7 fusion.10
  238.4 0.1 slice_multiply_fusion
  238.4 30.4 %all-gather = f32[256,512]{1,0:T(8,128)S(1)} all-gather(f32[32,512]{1,0:T(8,128)S(1)} %slice.28), channel_id=2, replica_groups=mesh['yh'=2,'x'=4,'core'=2,'z'=4,'yl'=2] {'z','yl'}, dimensions={0}, use_global_device_ids=true | all-gather | bytes 589824 | tf_op jit(solution)/shard_map/all_gather | solution.py:67
  268.9 0.6 broadcast_multiply_fusion
  269.5 0.9 mul.32
  270.4 0.0 copy-done.1
  (4 shorter events, 0.1 us)
Async XLA Ops:
  7.2 1.6 copy-start
  7.2 81.9 %reduce-scatter.3.cloned.1.call-start = ((), (), s32[]{:S(2)}) async-start(), calls=%async_computation.3 | async-start | bytes 6291456 | tf_op jit(solution)/shard_map/reduce_scatter | solution.py:54
  24.4 13.2 %copy-start.3 = (bf16[2,1024,512]{2,1,0:T(8,128)(2,1)S(1)}, bf16[2,1024,512]{2,1,0:T(8,128)(2,1)}, u32[]{:S(2)}) copy-start(bf16[2,1024,512]{2,1,0:T(8,128)(2,1)} %convolution_convert_fusion) | copy-start | bytes 6291460
  34.9 2.7 copy-start.2
  43.8 67.9 %reduce-scatter.5.cloned.1.call-start = ((), (), s32[]{:S(2)}) async-start(), calls=%async_computation.4 | async-start | bytes 14155776 | tf_op jit(solution)/shard_map/reduce_scatter | solution.py:55
  219.3 51.1 %copy-start.1 = (bf16[2,1024,512]{2,1,0:T(8,128)(2,1)S(1)}, bf16[2,1024,512]{2,1,0:T(8,128)(2,1)}, u32[]{:S(2)}) copy-start(bf16[2,1024,512]{2,1,0:T(8,128)(2,1)} %param.5) | copy-start | bytes 6291460
Sparse Core Ops, SparseCore 0:
  44.0 17.2 reduce-scatter.2
  89.2 22.5 reduce-scatter.4
